TPU v7x, 256 devices: a whole 4x4x8 slice. The times are simulated.
256 devices in a mesh: grp: 32 (over z, x), tp: 8 (over y, core).
Axes of the slice: x: 4, y: 4, z: 8, core: 2. Of those that a mesh axis runs over, the one named last changes fastest.
Arguments:
- tokens: bfloat16 [32768, 2048], P('grp'), may hold values from -6 to 6
- norm_gain: float32 [2048], replicated, may hold values from 0.5 to 7
- w_qkv: bfloat16 [2048, 3, 2048], P(None, None, 'tp'), may hold values from -0.125 to 0.125
- w_out: bfloat16 [2048, 2048], P('tp'), may hold values from -0.125 to 0.125
- a_in: bfloat16 [64, 2048, 48], P('grp', 'tp'), may hold values from -0.125 to 0.125
- b_in: bfloat16 [64, 3, 16, 2048], P('grp', None, None, 'tp'), may hold values from -1.5 to 1.5
- a_out: bfloat16 [64, 2048, 16], P('grp', 'tp'), may hold values from -0.125 to 0.125
- b_out: bfloat16 [64, 16, 2048], P('grp', None, 'tp'), may hold values from -1.5 to 1.5
- req_len: int32 [32, 4], replicated, may hold values from 1 to 512, 1024 in all within a row
- req_adapter: int32 [32, 4], replicated, may hold values from 0 to 63, as said below
- holder: int32 [64], replicated, may hold values from 0 to 63, each once
- page_table: int32 [32, 8], P('grp'), may hold values from 0 to 7, each once within a row
Outputs:
- layer_out: bfloat16 [32768, 2048], P('grp', 'tp')
- kv_pages: bfloat16 [256, 2, 128, 2048], P('grp', None, None, 'tp')
Inputs may be any that keep to these rules, and one draw needn't show every extreme that they name: `req_adapter`: exactly 16 different adapters appear among all requests.
All inputs are finite; a program needn't handle non-finite values.
Results may differ from a plain program's by a relative error of at most 0.017.
The roundings to bfloat16 on the way count: a program that leaves them out, or rounds other values in their place, can miss the bound.
Values may be sent and summed in bfloat16 or wider, within the bound.
No kernel may reach another device: no remote copies, remote signals or barrier semaphores. Data moves between devices by JAX's collectives and lax.ppermute only.
A program may use at most 128 MiB of HBM per device.

v0:
```python
import math
import jax
import jax.numpy as jnp
from jax import lax
from jax.sharding import PartitionSpec as P

HD = 128
PAGE = 128
EPSILON = 1e-05
THETA = 10000.0


def shifted(block, axis, distance):
    devices = range(lax.axis_size(axis))
    route = [(i - distance, i) for i in devices if i - distance in devices]
    return lax.ppermute(block, axis, route)


def rms_norm(token_rows, norm_gain):
    values = token_rows.astype(jnp.float32)
    norm_scale = lax.rsqrt(jnp.mean(values * values, axis=-1, keepdims=True) + EPSILON)
    return (values * norm_scale * norm_gain).astype(jnp.bfloat16)


def request_layout(lengths, offset, tok_count):
    end_at = jnp.cumsum(lengths)
    starts = end_at - lengths
    row_ids = jnp.arange(tok_count, dtype=jnp.int32)
    segment = jnp.sum((row_ids[:, None] >= end_at[None, :]).astype(jnp.int32), axis=1)
    member = segment[:, None] == jnp.arange(lengths.shape[0], dtype=jnp.int32)[None, :]
    begin_at = jnp.sum(jnp.where(member, starts[None, :], 0), axis=1)
    position = row_ids - begin_at + jnp.where(segment == 0, offset, 0)
    return (segment, member, position)


def rotate(head_rows, position, head_dim):
    half_dim = head_dim // 2
    frequency = THETA ** (-(jnp.arange(half_dim, dtype=jnp.float32) * (2.0 / head_dim)))
    angles = position.astype(jnp.float32)[:, None] * frequency[None, :]
    cosine = jnp.cos(angles)[:, None, :]
    sine_part = jnp.sin(angles)[:, None, :]
    lower_half = head_rows[..., :half_dim]
    upper_half = head_rows[..., half_dim:]
    return jnp.concatenate(
        [
            lower_half * cosine - upper_half * sine_part,
            upper_half * cosine + lower_half * sine_part,
        ],
        axis=-1,
    )


def local(
    tokens,
    norm_gain,
    w_qkv,
    w_out,
    a_in,
    b_in,
    a_out,
    b_out,
    req_len,
    req_adapter,
    holder,
    page_table,
):
    tok_count = tokens.shape[0]
    local_width = w_out.shape[0]
    local_heads = local_width // HD
    req_count = req_len.shape[1]
    rank_dim = a_out.shape[2]
    group_id = lax.axis_index("grp")
    tp_id = lax.axis_index("tp")
    lengths = lax.dynamic_index_in_dim(req_len, group_id, 0, keepdims=False)
    earlier = lax.dynamic_index_in_dim(req_len, jnp.maximum(group_id - 1, 0), 0, keepdims=False)
    continued = group_id > 0
    prev_len = earlier[req_count - 1]
    offset = jnp.where(continued, prev_len, 0)
    segment, member, position = request_layout(lengths, offset, tok_count)
    wanted = lax.dynamic_index_in_dim(req_adapter, group_id, 0, keepdims=False)
    stacks = (
        lax.all_gather(a_in, "grp", axis=0, tiled=True),
        lax.all_gather(b_in, "grp", axis=0, tiled=True),
        lax.all_gather(a_out, "grp", axis=0, tiled=True),
        lax.all_gather(b_out, "grp", axis=0, tiled=True),
    )
    req_slots = holder[wanted]
    sel_in = jnp.take(stacks[0], req_slots, axis=0)
    sel_up = jnp.take(stacks[1], req_slots, axis=0)
    sel_odown = jnp.take(stacks[2], req_slots, axis=0)
    sel_oup = jnp.take(stacks[3], req_slots, axis=0)
    member_f = member.astype(jnp.float32)
    pick_bf = member.astype(jnp.bfloat16)
    normed = rms_norm(tokens, norm_gain)
    own_cols = lax.dynamic_slice_in_dim(normed, tp_id * local_width, local_width, 1)
    down_f = jnp.einsum("td,rdk->trk", own_cols, sel_in, preferred_element_type=jnp.float32)
    lowrank_f = lax.psum(jnp.sum(down_f * member_f[:, :, None], axis=1), "tp")
    lowrank = lowrank_f.astype(jnp.bfloat16)
    spread = (pick_bf[:, :, None] * lowrank[:, None, :]).reshape(tok_count, req_count, 3, rank_dim)
    delta_qkv = jnp.einsum("trck,rckd->tcd", spread, sel_up, preferred_element_type=jnp.float32)
    base_qkv = jnp.dot(
        normed, w_qkv.reshape(w_qkv.shape[0], 3 * local_width), preferred_element_type=jnp.float32
    )
    qkv = (base_qkv.reshape(tok_count, 3, local_width) + delta_qkv).reshape(
        tok_count, 3, local_heads, HD
    )
    query_rows = rotate(qkv[:, 0], position, HD).astype(jnp.bfloat16)
    key_rows = rotate(qkv[:, 1], position, HD).astype(jnp.bfloat16).reshape(tok_count, local_width)
    value_rows = qkv[:, 2].astype(jnp.bfloat16).reshape(tok_count, local_width)
    row_ids = jnp.arange(tok_count, dtype=jnp.int32)
    far_key, far_value = shifted((key_rows, value_rows), "grp", 1)
    far_ok = continued & (segment[:, None] == 0) & (row_ids[None, :] >= tok_count - prev_len)
    far_count = far_key.shape[0]
    near_ok = (segment[:, None] == segment[None, :]) & (row_ids[None, :] <= row_ids[:, None])
    allowed = jnp.concatenate([far_ok, near_ok], axis=1)
    key_all = jnp.concatenate([far_key, key_rows], axis=0).reshape(
        far_count + tok_count, local_heads, HD
    )
    value_all = jnp.concatenate([far_value, value_rows], axis=0).reshape(
        far_count + tok_count, local_heads, HD
    )
    score_scale = 1.0 / math.sqrt(HD)
    scores = (
        jnp.einsum("thd,shd->hts", query_rows, key_all, preferred_element_type=jnp.float32)
        * score_scale
    )
    scores = jnp.where(allowed[None], scores, -jnp.inf)
    row_top = jnp.max(scores, axis=-1, keepdims=True)
    weights = jnp.exp(scores - row_top)
    weights_bf = (weights / jnp.sum(weights, axis=-1, keepdims=True)).astype(jnp.bfloat16)
    mixed_heads = jnp.einsum(
        "hts,shd->thd", weights_bf, value_all, preferred_element_type=jnp.float32
    )
    attended = mixed_heads.astype(jnp.bfloat16).reshape(tok_count, local_width)
    partial_value = jnp.dot(attended, w_out, preferred_element_type=jnp.float32)
    base_out = lax.psum_scatter(
        partial_value.astype(jnp.bfloat16), "tp", scatter_dimension=1, tiled=True
    ).astype(jnp.float32)
    down_o = jnp.einsum("td,rdk->trk", attended, sel_odown, preferred_element_type=jnp.float32)
    low_o = lax.psum(jnp.sum(down_o * member_f[:, :, None], axis=1).astype(jnp.bfloat16), "tp")
    spread_o = (pick_bf[:, :, None] * low_o[:, None, :]).reshape(tok_count, req_count * rank_dim)
    delta_o = jnp.dot(
        spread_o,
        sel_oup.reshape(req_count * rank_dim, local_width),
        preferred_element_type=jnp.float32,
    )
    own_rows = lax.dynamic_slice_in_dim(tokens, tp_id * local_width, local_width, 1).astype(
        jnp.float32
    )
    layer_out = (own_rows + base_out + delta_o).astype(jnp.bfloat16)
    page_row = page_table[0]
    page_count = page_row.shape[0]
    numbers = jnp.arange(page_count, dtype=jnp.int32)
    inverse = jnp.sum(jnp.where(page_row[:, None] == numbers[None, :], numbers[:, None], 0), axis=0)
    both_blocks = jnp.stack(
        [
            key_rows.reshape(page_count, PAGE, local_width),
            value_rows.reshape(page_count, PAGE, local_width),
        ],
        axis=1,
    )
    kv_pages = jnp.take(both_blocks, inverse, axis=0)
    return (layer_out, kv_pages)


def solution(mesh):
    return jax.shard_map(
        local,
        mesh=mesh,
        in_specs=(
            P("grp", None),
            P(),
            P(None, None, "tp"),
            P("tp", None),
            P("grp", "tp", None),
            P("grp", None, None, "tp"),
            P("grp", "tp", None),
            P("grp", None, "tp"),
            P(),
            P(),
            P(),
            P("grp", None),
        ),
        out_specs=(P("grp", "tp"), P("grp", None, None, "tp")),
        check_vma=False,
    )
```

profile of v0, /device:TPU:2, one launch (start us, length us, event | category | flops | bytes accessed | tf_op | source)
XLA Modules:
  0.0 358.6 jit_solution(400273009174848627)
XLA Ops:
  13.9 3.1 fusion.2
  17.6 4.7 %copy.40 = bf16[2048,3,256]{0,2,1:T(8,128)(2,1)} copy(bf16[2048,3,256]{2,0,1:T(8,128)(2,1)} %param.14) | data formatting | bytes 6291456 | tf_op args[2]
  22.3 3.0 multiply_cosine_fusion
  27.9 1.9 copy-done.3
  29.8 5.1 %fusion.9 = f32[1024,3,256]{0,2,1:T(8,128)} fusion(bf16[1024,2048]{1,0:T(8,128)(2,1)S(1)} %fusion.4, bf16[2048,3,256]{0,2,1:T(8,128)(2,1)S(1)} %copy-done.5), kind=kOutput, calls=%fused_computation.21 | convolution fusion | flops 3221225472 | bytes 10485760 | tf_op jit(solution)/shard_map/dot_general | solution.py:101
  34.9 54.5 %all-gather.5.cloned.1.call-done = bf16[64,256,48]{1,2,0:T(8,128)(2,1)} async-done(((bf16[2,256,48]{1,2,0:T(8,128)(2,1)}), bf16[64,256,48]{1,2,0:T(8,128)(2,1)}) %all-gather.5.cloned.1.call-update) | async-done | bytes 1572880 | tf_op jit(solution)/shard_map/all_gather | solution.py:82
  89.4 2.0 gather_fusion.2
  92.9 25.7 %all-reduce.1 = bf16[1024,48]{0,1:T(8,128)(2,1)S(1)} all-reduce(f32[1024,48]{0,1:T(8,128)S(1)} %multiply_reduce_fusion), channel_id=1, replica_groups=mesh['grp'=32,'tp'=8] {'tp'}, use_global_device_ids=true, to_apply=%region_4.5 | all-reduce | flops 49152 | bytes 294912 | tf_op jit(solution)/shard_map/psum | solution.py:97
  118.6 47.8 %all-gather.3.cloned.1.call-done = bf16[64,3,16,256]{3,2,1,0:T(8,128)(2,1)} async-done(((bf16[2,3,16,256]{3,2,1,0:T(8,128)(2,1)}), bf16[64,3,16,256]{3,2,1,0:T(8,128)(2,1)}) %all-gather.3.cloned.1.call-update) | async-done | bytes 1572880 | tf_op jit(solution)/shard_map/all_gather | solution.py:83
  166.4 2.0 gather_fusion.1
  168.4 2.6 bitcast_add_fusion
  174.3 3.5 collective-permute-start
  177.8 1.6 copy.55
  179.3 1.6 multiply_subtract_fusion
  182.3 3.2 collective-permute-start.1
  186.8 2.6 subtract_convert_fusion
  189.4 7.9 %collective-permute-done.1 = bf16[1024,256]{0,1:T(8,128)(2,1)} collective-permute-done((bf16[1024,256]{0,1:T(8,128)(2,1)}, bf16[1024,256]{0,1:T(8,128)(2,1)}, u32[]{:S(2)}, u32[]{:S(2)}) %collective-permute-start.1) | collective-permute-done | bytes 524320 | tf_op jit(solution)/shard_map/ppermute | solution.py:16
  198.6 10.8 %fusion.53 = (f32[2,1024]{1,0:T(2,128)S(1)}, f32[2,1024,2048]{2,1,0:T(8,128)}) fusion(pred[1024,2048]{1,0:T(8,128)(4,1)} %pad_add_fusion, bf16[1024,2,128]{2,0,1:T(8,128)(2,1)S(1)} %maximum_convert_fusion, bf16[1024,2,128]{2,0,1:T(8,128)(2,1)S(1)} %copy.45, bf16[1024,2,64]{2,0,1:T(8,128)(2,1)} %get-tuple-element.7, bf16[1024,2,64]{2,0,1:T(8,128)(2,1)} %get-tuple-element.6), kind=kOutput, calls=%fused_computation.109 | convolution fusion | flops 1093666816 | bytes 20455424 | tf_op jit(solution)/shard_map/sub | solution.py:129
  209.3 8.9 %fusion.17 = bf16[2,128,1024]{2,1,0:T(8,128)(2,1)S(1)} fusion(f32[2,1024,2048]{2,1,0:T(8,128)} %get-tuple-element.17, f32[2,1024]{1,0:T(2,128)S(1)} %get-tuple-element.16, bf16[1024,2,128]{0,2,1:T(8,128)(2,1)S(1)} %slice_bitcast_fusion, bf16[1024,2,128]{0,2,1:T(8,128)(2,1)} %bitcast.17), kind=kOutput, calls=%fused_computation.33 | convolution fusion | flops 1084489728 | bytes 18358272 | tf_op jit(solution)/shard_map/hts,shd->thd/dot_general | solution.py:131
  219.1 3.2 convolution_convert_fusion
  222.4 49.4 %all_gather.14 = bf16[64,256,16]{1,2,0:T(8,128)(2,1)S(1)} all-gather(bf16[2,256,16]{1,2,0:T(8,128)(2,1)S(1)} %copy-done.7), channel_id=1, replica_groups=mesh['grp'=32,'tp'=8] {'grp'}, dimensions={0}, use_global_device_ids=true | all-gather | bytes 540672 | tf_op jit(solution)/shard_map/all_gather | solution.py:84
  272.4 48.5 %all_gather.15 = bf16[64,16,256]{2,1,0:T(8,128)(2,1)S(1)} all-gather(bf16[2,16,256]{2,1,0:T(8,128)(2,1)S(1)} %copy-done.8), channel_id=1, replica_groups=mesh['grp'=32,'tp'=8] {'grp'}, dimensions={0}, use_global_device_ids=true | all-gather | bytes 540672 | tf_op jit(solution)/shard_map/all_gather | solution.py:85
  326.1 23.6 %psum.15 = bf16[1024,16]{0,1:T(8,128)(2,1)S(1)} all-reduce(bf16[1024,16]{0,1:T(8,128)(2,1)S(1)} %multiply_reduce_fusion.1), channel_id=1, replica_groups=mesh['grp'=32,'tp'=8] {'tp'}, use_global_device_ids=true, to_apply=%region_10.11 | all-reduce | flops 16384 | bytes 65536 | tf_op jit(solution)/shard_map/psum | solution.py:140
  349.7 2.3 fusion.16
  (78 shorter events, 23.7 us)
Async XLA Ops:
  7.2 211.9 %copy-start = (bf16[256,2048]{1,0:T(8,128)(2,1)S(1)}, bf16[256,2048]{1,0:T(8,128)(2,1)}, u32[]{:S(2)}) copy-start(bf16[256,2048]{1,0:T(8,128)(2,1)} %param.15) | copy-start | bytes 3145732
  7.2 82.2 %all-gather.5.cloned.1.call-start = ((), (), s32[]{:S(2)}) async-start(), calls=%async_computation.2 | async-start | bytes 1622016 | tf_op jit(solution)/shard_map/all_gather | solution.py:82
  7.9 158.5 %all-gather.3.cloned.1.call-start = ((), (), s32[]{:S(2)}) async-start(), calls=%async_computation.1 | async-start | bytes 1622016 | tf_op jit(solution)/shard_map/all_gather | solution.py:83
  8.7 341.0 %reduce-scatter.2.cloned.1.call-start = ((), (), s32[]{:S(2)}) async-start(), calls=%async_computation.3 | async-start | bytes 4718592 | tf_op jit(solution)/shard_map/reduce_scatter | solution.py:136
  22.3 4.6 %copy-start.9 = (f32[2048]{0:T(1024)S(1)}, f32[2048]{0:T(1024)}, u32[]{:S(2)}) copy-start(f32[2048]{0:T(1024)} %param.13) | copy-start | bytes 24580
  22.3 4.6 %copy-start.1 = (bf16[1024,2048]{1,0:T(8,128)(2,1)S(1)}, bf16[1024,2048]{1,0:T(8,128)(2,1)}, u32[]{:S(2)}) copy-start(bf16[1024,2048]{1,0:T(8,128)(2,1)} %param.12) | copy-start | bytes 12582916
  26.8 3.0 copy-start.5
  27.9 1.9 copy-start.3
  171.0 1.8 copy-start.2
  174.3 35.1 %collective-permute-start = (bf16[1024,256]{0,1:T(8,128)(2,1)}, bf16[1024,256]{0,1:T(8,128)(2,1)}, u32[]{:S(2)}, u32[]{:S(2)}) collective-permute-start(bf16[1024,256]{0,1:T(8,128)(2,1)} %bitcast.83), channel_id=1, source_target_pairs={{0,8},{8,16},{16,24},{24,32},{32,40},{40,48},{48,56},{56,64},{64,7... | collective-permute-start | bytes 1572872 | tf_op jit(solution)/shard_map/ppermute | solution.py:16
  182.3 14.9 %collective-permute-start.1 = (bf16[1024,256]{0,1:T(8,128)(2,1)}, bf16[1024,256]{0,1:T(8,128)(2,1)}, u32[]{:S(2)}, u32[]{:S(2)}) collective-permute-start(bf16[1024,256]{0,1:T(8,128)(2,1)} %bitcast.24), channel_id=1, source_target_pairs={{0,8},{8,16},{16,24},{24,32},{32,40},{40,48},{48,56},{56,64},{64,7... | collective-permute-start | bytes 1572872 | tf_op jit(solution)/shard_map/ppermute | solution.py:16
  218.3 0.8 copy-start.4
  219.1 3.3 copy-start.7
  222.3 50.0 %copy-start.8 = (bf16[2,16,256]{2,1,0:T(8,128)(2,1)S(1)}, bf16[2,16,256]{2,1,0:T(8,128)(2,1)}, u32[]{:S(2)}) copy-start(bf16[2,16,256]{2,1,0:T(8,128)(2,1)} %param.19) | copy-start | bytes 49156
  222.3 99.1 %copy-start.10 = (s32[1,8]{1,0:T(1,128)S(1)}, s32[1,8]{1,0:T(1,128)}, u32[]{:S(2)}) copy-start(s32[1,8]{1,0:T(1,128)} %param.23) | copy-start | bytes 100
  222.3 99.8 %copy-start.6 = (bf16[1024,1,2,128]{0,3,2,1:T(8,128)(2,1)S(1)}, bf16[1024,1,2,128]{0,3,2,1:T(8,128)(2,1)}, u32[]{:S(2)}) copy-start(bf16[1024,1,2,128]{0,3,2,1:T(8,128)(2,1)} %slice.61) | copy-start | bytes 1572868
Sparse Core Ops, SparseCore 0:
  10.6 78.7 all-gather.4
  92.0 74.4 all-gather.2
  222.5 41.1 reduce-scatter.1
where the time goes:
time: 359 us
  blocking collectives  147 us (41%)
  waiting for transfers between devices  112 us (31%)
  matrix products  35.6 us (10%)
  local copies, waits for them, and re-layouts  25.7 us (7%)
  other arithmetic  16.4 us (5%)
  between operations  15.4 us (4%)
  starting transfers between devices  6.77 us (2%)
    all_gather x1, waiting for transfers between devices, local(): lax.all_gather(a_in, 'grp', axis=0, tiled=True)  54.5 us
    all_gather x1, blocking collectives, local(): lax.all_gather(a_out, 'grp', axis=0, tiled=True)  49.4 us
    all_gather x1, blocking collectives, local(): lax.all_gather(b_out, 'grp', axis=0, tiled=True)  48.5 us
    all_gather x1, waiting for transfers between devices, local(): lax.all_gather(b_in, 'grp', axis=0, tiled=True)  47.8 us
    psum x1, blocking collectives, local(): lowrank_f = lax.psum(jnp.sum(down_f * member_f[:, :, None], axis=1), 'tp')  25.7 us
    psum x1, blocking collectives, local(): lax.psum(jnp.sum(down_o * member_f[:, :, None], axis=1).astype(jnp.bfloat...  23.6 us
    sub x1, matrix products, local(): weights = jnp.exp(scores - row_top)  10.8 us
    unnamed x27, local copies, waits for them, and re-layouts  10.4 us
  transfers between devices with their start and end apart: 5, of which 3 were waited for; matrix products, arithmetic and copies ran while one was open for 15% of the time, Pallas kernels for 0%

commit v1 on v0

--- a/solution.py
+++ b/solution.py
@@ -81,7 +81,9 @@
     stacks = (
         lax.all_gather(a_in, "grp", axis=0, tiled=True),
         lax.all_gather(b_in, "grp", axis=0, tiled=True),
-        lax.all_gather(a_out, "grp", axis=0, tiled=True),
+        jnp.concatenate(
+            lax.all_to_all(jnp.stack([a_out] * lax.axis_size("grp")), "grp", 0, 0), axis=0
+        ),
         lax.all_gather(b_out, "grp", axis=0, tiled=True),
     )
     req_slots = holder[wanted]

time: 359 us -> 329 us (0.916)
  blocking collectives: 147 us -> 105 us
  starting transfers between devices: 6.77 us -> 16.1 us
    all_gather x1 -> x0, blocking collectives: 49.4 us -> none  [local(): lax.all_gather(a_out, 'grp', axis=0, tiled=True)]
    all_to_all x0 -> x1, starting transfers between devices: none -> 9.31 us  [local(): lax.all_to_all(jnp.stack([a_out] * lax.axis_size('grp')), 'grp', 0, 0)]
    all_gather x1, blocking collectives: 48.5 us -> 55.7 us  [local(): lax.all_gather(b_out, 'grp', axis=0, tiled=True)]
  transfers between devices with their start and end apart: 5 -> 6, of which waited for: 3 -> 3; matrix products, arithmetic and copies ran while one was open for 15% -> 17% of each run, Pallas kernels for 0% -> 0%
where the time goes in v1:
time: 329 us; the launch traced here: 328 us
  waiting for transfers between devices  112 us (34%)
  blocking collectives  105 us (32%)
  matrix products  35.6 us (11%)
  local copies, waits for them, and re-layouts  27.6 us (8%)
  other arithmetic  16.4 us (5%)
  starting transfers between devices  16.1 us (5%)
  between operations  15.4 us (5%)
    all_gather x1, blocking collectives, local(): lax.all_gather(b_out, 'grp', axis=0, tiled=True)  55.7 us
    all_gather x1, waiting for transfers between devices, local(): lax.all_gather(a_in, 'grp', axis=0, tiled=True)  54.5 us
    all_gather x1, waiting for transfers between devices, local(): lax.all_gather(b_in, 'grp', axis=0, tiled=True)  47.8 us
    psum x1, blocking collectives, local(): lowrank_f = lax.psum(jnp.sum(down_f * member_f[:, :, None], axis=1), 'tp')  25.7 us
    psum x1, blocking collectives, local(): lax.psum(jnp.sum(down_o * member_f[:, :, None], axis=1).astype(jnp.bfloat...  23.6 us
    sub x1, matrix products, local(): weights = jnp.exp(scores - row_top)  10.8 us
    unnamed x27, local copies, waits for them, and re-layouts  10.4 us
    all_to_all x1, starting transfers between devices, local(): lax.all_to_all(jnp.stack([a_out] * lax.axis_size('grp')), 'grp', 0, 0)  9.31 us
  transfers between devices with their start and end apart: 6, of which 3 were waited for; matrix products, arithmetic and copies ran while one was open for 17% of the time, Pallas kernels for 0%

profile of v1, /device:TPU:2, one launch (start us, length us, event | category | flops | bytes accessed | tf_op | source)
XLA Modules:
  0.0 327.6 jit_solution(14673971827651407381)
XLA Ops:
  13.9 3.1 fusion.2
  17.6 4.7 %copy.42 = bf16[2048,3,256]{0,2,1:T(8,128)(2,1)} copy(bf16[2048,3,256]{2,0,1:T(8,128)(2,1)} %param.14) | data formatting | bytes 6291456 | tf_op args[2]
  22.3 3.0 multiply_cosine_fusion
  27.9 1.9 copy-done.3
  29.8 5.1 %fusion.9 = f32[1024,3,256]{0,2,1:T(8,128)} fusion(bf16[1024,2048]{1,0:T(8,128)(2,1)S(1)} %fusion.4, bf16[2048,3,256]{0,2,1:T(8,128)(2,1)S(1)} %copy-done.5), kind=kOutput, calls=%fused_computation.21 | convolution fusion | flops 3221225472 | bytes 10485760 | tf_op jit(solution)/shard_map/dot_general | solution.py:103
  34.9 54.5 %all-gather.5.cloned.1.call-done = bf16[64,256,48]{1,2,0:T(8,128)(2,1)} async-done(((bf16[2,256,48]{1,2,0:T(8,128)(2,1)}), bf16[64,256,48]{1,2,0:T(8,128)(2,1)}) %all-gather.5.cloned.1.call-update) | async-done | bytes 1572880 | tf_op jit(solution)/shard_map/all_gather | solution.py:82
  89.4 2.0 gather_fusion.2
  92.9 25.7 %all-reduce.1 = bf16[1024,48]{0,1:T(8,128)(2,1)S(1)} all-reduce(f32[1024,48]{0,1:T(8,128)S(1)} %multiply_reduce_fusion), channel_id=1, replica_groups=mesh['grp'=32,'tp'=8] {'tp'}, use_global_device_ids=true, to_apply=%region_4.5 | all-reduce | flops 49152 | bytes 294912 | tf_op jit(solution)/shard_map/psum | solution.py:99
  118.6 47.8 %all-gather.3.cloned.1.call-done = bf16[64,3,16,256]{3,2,1,0:T(8,128)(2,1)} async-done(((bf16[2,3,16,256]{3,2,1,0:T(8,128)(2,1)}), bf16[64,3,16,256]{3,2,1,0:T(8,128)(2,1)}) %all-gather.3.cloned.1.call-update) | async-done | bytes 1572880 | tf_op jit(solution)/shard_map/all_gather | solution.py:83
  166.4 2.0 gather_fusion.1
  168.4 2.6 bitcast_add_fusion
  174.3 3.5 %collective-permute-start = (bf16[1024,256]{0,1:T(8,128)(2,1)}, bf16[1024,256]{0,1:T(8,128)(2,1)}, u32[]{:S(2)}, u32[]{:S(2)}) collective-permute-start(bf16[1024,256]{0,1:T(8,128)(2,1)} %bitcast.84), channel_id=1, source_target_pairs={{0,8},{8,16},{16,24},{24,32},{32,40},{40,48},{48,56},{56,64},{64,7... | collective-permute-start | bytes 1572872 | tf_op jit(solution)/shard_map/ppermute | solution.py:16
  179.3 1.6 multiply_subtract_fusion
  182.3 3.2 collective-permute-start.1
  186.8 2.6 subtract_convert_fusion
  189.4 7.9 %collective-permute-done.1 = bf16[1024,256]{0,1:T(8,128)(2,1)} collective-permute-done((bf16[1024,256]{0,1:T(8,128)(2,1)}, bf16[1024,256]{0,1:T(8,128)(2,1)}, u32[]{:S(2)}, u32[]{:S(2)}) %collective-permute-start.1) | collective-permute-done | bytes 524320 | tf_op jit(solution)/shard_map/ppermute | solution.py:16
  198.6 10.8 %fusion.53 = (f32[2,1024]{1,0:T(2,128)S(1)}, f32[2,1024,2048]{2,1,0:T(8,128)}) fusion(pred[1024,2048]{1,0:T(8,128)(4,1)} %pad_add_fusion, bf16[1024,2,128]{2,0,1:T(8,128)(2,1)S(1)} %maximum_convert_fusion, bf16[1024,2,128]{2,0,1:T(8,128)(2,1)S(1)} %copy.47, bf16[1024,2,64]{2,0,1:T(8,128)(2,1)} %get-tuple-element.7, bf16[1024,2,64]{2,0,1:T(8,128)(2,1)} %get-tuple-element.6), kind=kOutput, calls=%fused_computation.109 | convolution fusion | flops 1093666816 | bytes 20455424 | tf_op jit(solution)/shard_map/sub | solution.py:131
  209.3 8.9 %fusion.17 = bf16[2,128,1024]{2,1,0:T(8,128)(2,1)S(1)} fusion(f32[2,1024,2048]{2,1,0:T(8,128)} %get-tuple-element.17, f32[2,1024]{1,0:T(2,128)S(1)} %get-tuple-element.16, bf16[1024,2,128]{0,2,1:T(8,128)(2,1)S(1)} %slice_bitcast_fusion, bf16[1024,2,128]{0,2,1:T(8,128)(2,1)} %bitcast.17), kind=kOutput, calls=%fused_computation.33 | convolution fusion | flops 1084489728 | bytes 18358272 | tf_op jit(solution)/shard_map/hts,shd->thd/dot_general | solution.py:133
  219.1 3.2 convolution_convert_fusion
  223.2 9.3 %all-to-all-start = ((bf16[32,2,256,16]{2,3,1,0:T(8,128)(2,1)}), bf16[32,2,256,16]{2,3,1,0:T(8,128)(2,1)S(1)}, u32[]{:S(2)}, u32[]{:S(2)}) async-start(bf16[32,2,256,16]{2,3,1,0:T(8,128)(2,1)} %stack.4), calls=%async_computation.1 | async-start | bytes 1048576 | tf_op jit(solution)/shard_map/all_to_all | solution.py:85
  232.6 55.7 %all_gather.11 = bf16[64,16,256]{2,1,0:T(8,128)(2,1)} all-gather(bf16[2,16,256]{2,1,0:T(8,128)(2,1)S(1)} %copy-done.8), channel_id=1, replica_groups=mesh['grp'=32,'tp'=8] {'grp'}, dimensions={0}, use_global_device_ids=true | all-gather | bytes 540672 | tf_op jit(solution)/shard_map/all_gather | solution.py:87
  288.3 1.6 gather_fusion.4
  295.1 23.6 %psum.15 = bf16[1024,16]{0,1:T(8,128)(2,1)S(1)} all-reduce(bf16[1024,16]{0,1:T(8,128)(2,1)S(1)} %multiply_reduce_fusion.1), channel_id=1, replica_groups=mesh['grp'=32,'tp'=8] {'tp'}, use_global_device_ids=true, to_apply=%region_10.11 | all-reduce | flops 16384 | bytes 65536 | tf_op jit(solution)/shard_map/psum | solution.py:142
  318.8 2.3 fusion.16
  (80 shorter events, 25.6 us)
Async XLA Ops:
  7.2 211.9 %copy-start = (bf16[256,2048]{1,0:T(8,128)(2,1)S(1)}, bf16[256,2048]{1,0:T(8,128)(2,1)}, u32[]{:S(2)}) copy-start(bf16[256,2048]{1,0:T(8,128)(2,1)} %param.15) | copy-start | bytes 3145732
  7.2 82.2 %all-gather.5.cloned.1.call-start = ((), (), s32[]{:S(2)}) async-start(), calls=%async_computation.3 | async-start | bytes 1622016 | tf_op jit(solution)/shard_map/all_gather | solution.py:82
  7.9 158.5 %all-gather.3.cloned.1.call-start = ((), (), s32[]{:S(2)}) async-start(), calls=%async_computation.2 | async-start | bytes 1622016 | tf_op jit(solution)/shard_map/all_gather | solution.py:83
  8.7 310.1 %reduce-scatter.2.cloned.1.call-start = ((), (), s32[]{:S(2)}) async-start(), calls=%async_computation.4 | async-start | bytes 4718592 | tf_op jit(solution)/shard_map/reduce_scatter | solution.py:138
  22.3 4.6 %copy-start.9 = (f32[2048]{0:T(1024)S(1)}, f32[2048]{0:T(1024)}, u32[]{:S(2)}) copy-start(f32[2048]{0:T(1024)} %param.13) | copy-start | bytes 24580
  22.3 4.6 %copy-start.1 = (bf16[1024,2048]{1,0:T(8,128)(2,1)S(1)}, bf16[1024,2048]{1,0:T(8,128)(2,1)}, u32[]{:S(2)}) copy-start(bf16[1024,2048]{1,0:T(8,128)(2,1)} %param.12) | copy-start | bytes 12582916
  26.8 3.0 copy-start.5
  27.9 1.9 copy-start.3
  171.0 1.8 copy-start.2
  174.3 35.1 %collective-permute-start = (bf16[1024,256]{0,1:T(8,128)(2,1)}, bf16[1024,256]{0,1:T(8,128)(2,1)}, u32[]{:S(2)}, u32[]{:S(2)}) collective-permute-start(bf16[1024,256]{0,1:T(8,128)(2,1)} %bitcast.84), channel_id=1, source_target_pairs={{0,8},{8,16},{16,24},{24,32},{32,40},{40,48},{48,56},{56,64},{64,7... | collective-permute-start | bytes 1572872 | tf_op jit(solution)/shard_map/ppermute | solution.py:16
  182.3 14.9 %collective-permute-start.1 = (bf16[1024,256]{0,1:T(8,128)(2,1)}, bf16[1024,256]{0,1:T(8,128)(2,1)}, u32[]{:S(2)}, u32[]{:S(2)}) collective-permute-start(bf16[1024,256]{0,1:T(8,128)(2,1)} %bitcast.24), channel_id=1, source_target_pairs={{0,8},{8,16},{16,24},{24,32},{32,40},{40,48},{48,56},{56,64},{64,7... | collective-permute-start | bytes 1572872 | tf_op jit(solution)/shard_map/ppermute | solution.py:16
  218.3 0.8 copy-start.4
  219.1 3.3 copy-start.7
  222.3 10.2 %copy-start.8 = (bf16[2,16,256]{2,1,0:T(8,128)(2,1)S(1)}, bf16[2,16,256]{2,1,0:T(8,128)(2,1)}, u32[]{:S(2)}) copy-start(bf16[2,16,256]{2,1,0:T(8,128)(2,1)} %param.19) | copy-start | bytes 49156
  222.3 67.6 %copy-start.10 = (s32[1,8]{1,0:T(1,128)S(1)}, s32[1,8]{1,0:T(1,128)}, u32[]{:S(2)}) copy-start(s32[1,8]{1,0:T(1,128)} %param.23) | copy-start | bytes 100
  222.4 68.9 %copy-start.6 = (bf16[1024,1,2,128]{0,3,2,1:T(8,128)(2,1)S(1)}, bf16[1024,1,2,128]{0,3,2,1:T(8,128)(2,1)}, u32[]{:S(2)}) copy-start(bf16[1024,1,2,128]{0,3,2,1:T(8,128)(2,1)} %slice.61) | copy-start | bytes 1572868
  223.2 66.8 %all-to-all-start = ((bf16[32,2,256,16]{2,3,1,0:T(8,128)(2,1)}), bf16[32,2,256,16]{2,3,1,0:T(8,128)(2,1)S(1)}, u32[]{:S(2)}, u32[]{:S(2)}) async-start(bf16[32,2,256,16]{2,3,1,0:T(8,128)(2,1)} %stack.4), calls=%async_computation.1 | async-start | bytes 1048576 | tf_op jit(solution)/shard_map/all_to_all | solution.py:85
Sparse Core Ops, SparseCore 0:
  10.6 78.7 all-gather.4
  92.0 74.4 all-gather.2
  222.5 41.2 reduce-scatter.1
